TPU v7x, 128 devices: a whole 4x4x4 slice. The times are simulated.
128 devices in a mesh: seq: 64 (over z, x, y_lo, core), chan: 2 (over y_hi).
Axes of the slice: x: 4, y: 4 (y_hi: 2, y_lo: 2; y = y_hi * 2 + y_lo), z: 4, core: 2. Of those that a mesh axis runs over, the one named last changes fastest.
Arguments:
- signal: bfloat16 [2, 32768, 128], P('chan', 'seq'), may hold values from -6 to 6
- cotangent: bfloat16 [2, 32768, 128], P('chan', 'seq'), may hold values from -6 to 6
- band_freq: int32 [16], replicated, may hold values from 1 to 8191
- w_embed: float32 [32, 64], replicated, may hold values from -2 to 2
- b_embed: float32 [64], replicated, may hold values from -3.140625 to 3.140625
- w_out: float32 [64, 128], P(None, 'chan'), may hold values from -0.75 to 0.75
- decay: float32 [128], P('chan'), may hold values from 0.25 to 16, as said below
Outputs:
- conv_out: bfloat16 [2, 32768, 128], P('chan', 'seq')
- d_signal: bfloat16 [2, 32768, 128], P('chan', 'seq')
- grad_embed: float32 [32, 64], replicated
- grad_bias: float32 [64], replicated
- grad_out: float32 [64, 128], P(None, 'chan')
Inputs may be any that keep to these rules, and one draw needn't show every extreme that they name: decay rates are positive.
All inputs are finite; a program needn't handle non-finite values.
Results may differ from a plain program's by a relative error of at most 0.007.
Values may be sent and summed in bfloat16 or wider, within the bound.
No kernel may reach another device: no remote copies, remote signals or barrier semaphores. Data moves between devices by JAX's collectives and lax.ppermute only.
A program may use at most 192 MiB of HBM per device.

v0:
```python
import math
import jax
import jax.numpy as jnp
from jax import lax
from jax.sharding import PartitionSpec as P

exact_mode = lax.Precision.HIGHEST


def mat_dot(lhs_mat, rhs_mat):
    return jnp.dot(lhs_mat, rhs_mat, preferred_element_type=jnp.float32, precision=exact_mode)


def band_phase(band_freq, places, seq_total):
    upper_part = places // 1024
    lower_part = places % 1024
    partial_turn = upper_part[:, None] * band_freq[None, :] % seq_total
    wrapped = (partial_turn * 1024 + lower_part[:, None] * band_freq[None, :]) % seq_total
    return wrapped.astype(jnp.float32) * (2.0 * math.pi / seq_total)


def filter_parts(places, band_freq, w_embed, b_embed, w_out, decay, seq_total):
    phases = band_phase(band_freq, places, seq_total)
    features = jnp.concatenate([jnp.cos(phases), jnp.sin(phases)], axis=1)
    preact = mat_dot(features, w_embed) + b_embed[None, :]
    hidden = jnp.sin(preact)
    fraction = places.astype(jnp.float32) / seq_total
    envelope = (
        jnp.exp(-decay[None, :] * fraction[:, None]) * jnp.sqrt((1.0 + decay) / seq_total)[None, :]
    )
    taps = mat_dot(hidden, w_out) * envelope
    return (features, preact, hidden, taps, envelope)


def angle_table(rows_idx, cols_idx, modulus):
    wrapped = rows_idx[:, None] * cols_idx[None, :] % modulus
    angles = wrapped.astype(jnp.float32) * (2.0 * math.pi / modulus)
    return (jnp.cos(angles), jnp.sin(angles))


def local(signal, cotangent, band_freq, w_embed, b_embed, w_out, decay):
    devices = lax.axis_size("seq")
    rank_seq = lax.axis_index("seq")
    seg_len = signal.shape[1] * 2
    channels = signal.shape[2] // 2
    block_w = seg_len // devices
    width = block_w * channels
    rows_all = 2 * devices
    pair = rows_all // devices
    seq_total = seg_len * devices
    fft_size = 2 * seq_total
    inv_scale = 1.0 / fft_size
    n_arr = 3
    dev_ids = jnp.arange(devices, dtype=jnp.int32)
    row_ids = jnp.arange(rows_all, dtype=jnp.int32)
    blk_ids = jnp.arange(block_w, dtype=jnp.int32)
    lane_blk = jnp.arange(width, dtype=jnp.int32) // channels
    b_lane = rank_seq * block_w + lane_blk
    src = jnp.stack([signal.reshape(devices, width), cotangent.reshape(devices, width)], axis=1)
    cols = lax.all_to_all(src, "seq", split_axis=0, concat_axis=0, tiled=True)
    places = (dev_ids[:, None] * seg_len + rank_seq * block_w + blk_ids[None, :]).reshape(-1)
    features, preact, hidden, taps, envelope = filter_parts(
        places, band_freq, w_embed, b_embed, w_out, decay, seq_total
    )
    stacked = jnp.concatenate(
        [cols.astype(jnp.float32), taps.reshape(devices, 1, width)], axis=1
    ).reshape(devices, n_arr * width)
    col_cos, col_sin = angle_table(row_ids, dev_ids, rows_all)
    y_re = mat_dot(col_cos, stacked).reshape(rows_all, n_arr, width)
    y_im = -mat_dot(col_sin, stacked).reshape(rows_all, n_arr, width)
    tw_cos, tw_sin = angle_table(row_ids, b_lane, fft_size)
    tw_cos = tw_cos[:, None, :]
    tw_sin = tw_sin[:, None, :]
    t_re = y_re * tw_cos + y_im * tw_sin
    t_im = y_im * tw_cos - y_re * tw_sin
    spec = jnp.stack([t_re, t_im], axis=1)
    spec = lax.all_to_all(spec, "seq", split_axis=0, concat_axis=0, tiled=True)
    q_cos, q_sin = angle_table(dev_ids, dev_ids, devices)
    stage_a = mat_dot(jnp.concatenate([q_cos, q_sin], axis=0), spec.reshape(devices, -1))
    stage_a = stage_a.reshape(2, devices, pair, 2, n_arr, width)
    a_re = stage_a[0, :, :, 0] + stage_a[1, :, :, 1]
    a_im = stage_a[0, :, :, 1] - stage_a[1, :, :, 0]
    mid_cos, mid_sin = angle_table(dev_ids, lane_blk, seg_len)
    mid_cos = mid_cos[:, None, None, :]
    mid_sin = mid_sin[:, None, None, :]
    b_re = (a_re * mid_cos + a_im * mid_sin).reshape(devices, pair, n_arr, block_w, channels)
    b_im = (a_im * mid_cos - a_re * mid_sin).reshape(devices, pair, n_arr, block_w, channels)
    m_cos, m_sin = angle_table(blk_ids, blk_ids, block_w)

    def blk_mix(table, vals):
        return jnp.einsum(
            "mb,qkzbc->qkzmc", table, vals, preferred_element_type=jnp.float32, precision=exact_mode
        )

    s_re = blk_mix(m_cos, b_re) + blk_mix(m_sin, b_im)
    s_im = blk_mix(m_cos, b_im) - blk_mix(m_sin, b_re)
    sig_r, cot_r, tap_r = (s_re[:, :, 0], s_re[:, :, 1], s_re[:, :, 2])
    sig_i, cot_i, tap_i = (s_im[:, :, 0], s_im[:, :, 1], s_im[:, :, 2])
    prod_r = jnp.stack(
        [
            sig_r * tap_r - sig_i * tap_i,
            cot_r * tap_r + cot_i * tap_i,
            cot_r * sig_r + cot_i * sig_i,
        ],
        axis=2,
    )
    prod_i = jnp.stack(
        [
            sig_r * tap_i + sig_i * tap_r,
            cot_i * tap_r - cot_r * tap_i,
            cot_i * sig_r - cot_r * sig_i,
        ],
        axis=2,
    )
    u_re = blk_mix(m_cos, prod_r) - blk_mix(m_sin, prod_i)
    u_im = blk_mix(m_cos, prod_i) + blk_mix(m_sin, prod_r)
    u_re = u_re.reshape(devices, pair, n_arr, width)
    u_im = u_im.reshape(devices, pair, n_arr, width)
    v_re = u_re * mid_cos - u_im * mid_sin
    v_im = u_im * mid_cos + u_re * mid_sin
    v_all = jnp.stack([v_re, v_im]).reshape(2 * devices, -1)
    inv_mat = jnp.concatenate(
        [jnp.concatenate([q_cos, -q_sin], axis=1), jnp.concatenate([q_sin, q_cos], axis=1)], axis=0
    )
    w_all = mat_dot(inv_mat, v_all).reshape(2, devices, pair, n_arr, width)
    b_rows = dev_ids[:, None] * block_w + lane_blk[None, :]
    k1_own = rank_seq * pair + jnp.arange(pair, dtype=jnp.int32)
    ex_ang = b_rows[:, None, :] * k1_own[None, :, None] % fft_size
    ex_ang = ex_ang.astype(jnp.float32) * (2.0 * math.pi / fft_size)
    ex_cos = jnp.cos(ex_ang)[:, :, None, :]
    ex_sin = jnp.sin(ex_ang)[:, :, None, :]
    x_re = w_all[0] * ex_cos - w_all[1] * ex_sin
    x_im = w_all[0] * ex_sin + w_all[1] * ex_cos
    back = jnp.stack([x_re, x_im], axis=1)
    back = lax.all_to_all(back, "seq", split_axis=0, concat_axis=0, tiled=True)
    back = back.reshape(devices, 2, pair, n_arr * width)
    back = jnp.transpose(back, (1, 0, 2, 3)).reshape(2 * rows_all, n_arr * width)
    out_mat = jnp.concatenate([col_cos.T, -col_sin.T], axis=1)
    res = (mat_dot(out_mat, back) * inv_scale).reshape(devices, n_arr, width)
    rows_out = lax.all_to_all(
        res[:, 0:2].astype(jnp.bfloat16), "seq", split_axis=0, concat_axis=0, tiled=True
    )
    conv_out = rows_out[:, 0].reshape(1, seg_len // 2, 2 * channels)
    d_signal = rows_out[:, 1].reshape(1, seg_len // 2, 2 * channels)
    d_taps = res[:, 2].reshape(devices * block_w, channels)
    d_raw = d_taps * envelope
    d_preact = mat_dot(d_raw, w_out.T) * jnp.cos(preact)
    out_part = mat_dot(hidden.T, d_raw)
    embed_part = mat_dot(features.T, d_preact)
    bias_part = jnp.sum(d_preact, axis=0)
    out_sum = lax.psum(out_part, "seq")
    embed_all, bias_all = lax.psum((embed_part, bias_part), ("seq", "chan"))
    norm_scale = 1.0 / math.sqrt(seq_total)
    return (conv_out, d_signal, embed_all * norm_scale, bias_all * norm_scale, out_sum * norm_scale)


def solution(mesh):
    return jax.shard_map(
        local,
        mesh=mesh,
        in_specs=(
            P("chan", "seq", None),
            P("chan", "seq", None),
            P(),
            P(),
            P(),
            P(None, "chan"),
            P("chan"),
        ),
        out_specs=(P("chan", "seq", None), P("chan", "seq", None), P(), P(), P(None, "chan")),
        check_vma=False,
    )
```

profile of v0, /device:TPU:0, one launch (start us, length us, event | category | flops | bytes accessed | tf_op | source)
XLA Modules:
  0.0 615.8 jit_solution(7838954913175535610)
XLA Ops:
  4.4 9.9 %all-to-all-start = ((bf16[64,2,1024]{2,1,0:T(2,128)(2,1)}), bf16[64,2,1024]{2,1,0:T(2,128)(2,1)S(1)}, u32[]{:S(2)}, u32[]{:S(2)}) async-start(bf16[64,2,1024]{2,1,0:T(2,128)(2,1)} %pad_maximum_fusion.14), calls=%async_computation | async-start | bytes 524288 | tf_op jit(solution)/shard_map/all_to_all | solution.py:60
  29.3 4.1 copy.76
  33.4 6.9 %all-to-all-start.1 = ((f32[128,2,3,1024]{3,1,2,0:T(2,128)}), f32[128,2,3,1024]{3,1,2,0:T(2,128)S(1)}, u32[]{:S(2)}, u32[]{:S(2)}) async-start(f32[128,2,3,1024]{3,1,2,0:T(2,128)} %copy.76), calls=%async_computation.1 | async-start | bytes 6291456 | tf_op jit(solution)/shard_map/all_to_all | solution.py:77
  47.2 9.5 %fusion.38 = (f32[64,2,1024]{2,1,0:T(2,128)}, f32[64,2,1024]{2,1,0:T(2,128)}) fusion(s32[2]{0:T(128)S(1)} %iota_add_fusion.1, s32[64,1024]{1,0:T(8,128)S(1)} %broadcast_add_fusion), kind=kLoop, calls=%fused_computation.88 | loop fusion | flops 1835008 | bytes 1310728 | tf_op jit(solution)/shard_map/cos | solution.py:130
  56.8 23.2 %all-to-all-done.1 = f32[128,2,3,1024]{3,1,2,0:T(2,128)S(1)} async-done(((f32[128,2,3,1024]{3,1,2,0:T(2,128)}), f32[128,2,3,1024]{3,1,2,0:T(2,128)S(1)}, u32[]{:S(2)}, u32[]{:S(2)}) %all-to-all-start.1) | async-done | bytes 3145760 | tf_op jit(solution)/shard_map/all_to_all | solution.py:77
  83.7 4.3 reshape.397
  91.8 9.4 %fusion = f32[2,64,2,2,3,1024]{5,1,4,3,2,0:T(8,128)S(1)} fusion(f32[2,64,64,1,1,1]{2,1,5,4,3,0:T(8,128)} %bitcast.98, f32[2,2,3,1024,64]{3,2,1,0,4:T(4,128)} %dot_general.72), kind=kOutput, calls=%fused_computation.6 | convolution fusion | flops 1207959552 | bytes 9469952 | tf_op jit(solution)/shard_map/dot_general | solution.py:11
  110.0 5.5 fusion.51
  132.9 4.7 subtract_bitcast_fusion
  137.6 4.9 reshape.411
  142.5 6.4 %add_bitcast_fusion = f32[64,2,3,16,64]{4,3,2,1,0:T(8,128)} fusion(f32[64,2,3,64,16]{3,4,2,1,0:T(8,128)S(1)} %fusion.3, f32[64,2,1,16,64]{4,3,2,1,0:T(8,128)} %copy-done.5, f32[64,2,1,16,64]{4,3,2,1,0:T(8,128)} %copy-done.6, f32[64,2,1,16,64]{4,3,2,1,0:T(8,128)} %copy-done.4), kind=kOutput, calls=%fused_computation.9 | convolution fusion | flops 76680704 | bytes 4718592 | tf_op jit(solution)/shard_map/mb,qkzbc->qkzmc/dot_general | solution.py:91
  148.9 4.6 reshape.412
  157.1 4.1 copy.85
  161.2 5.0 reshape.400
  174.9 3.9 squeeze.5
  182.9 4.7 copy.86
  187.5 6.6 %all-to-all-start.2 = ((f32[64,2,2,3,1024]{4,2,3,1,0:T(2,128)}), f32[64,2,2,3,1024]{4,2,3,1,0:T(2,128)S(1)}, u32[]{:S(2)}, u32[]{:S(2)}) async-start(f32[64,2,2,3,1024]{4,2,3,1,0:T(2,128)} %copy.86), calls=%async_computation.2 | async-start | bytes 6291456 | tf_op jit(solution)/shard_map/all_to_all | solution.py:135
  194.9 38.9 %all-to-all-done.2 = f32[64,2,2,3,1024]{4,2,3,1,0:T(2,128)S(1)} async-done(((f32[64,2,2,3,1024]{4,2,3,1,0:T(2,128)}), f32[64,2,2,3,1024]{4,2,3,1,0:T(2,128)S(1)}, u32[]{:S(2)}, u32[]{:S(2)}) %all-to-all-start.2) | async-done | bytes 3145760 | tf_op jit(solution)/shard_map/all_to_all | solution.py:135
  237.4 5.0 reshape.401
  242.3 4.1 copy.88
  246.4 3.9 reshape.402
  259.9 64.6 %all-reduce = (f32[32,64]{1,0:T(8,128)S(1)}, f32[64]{0:T(128)S(1)}) all-reduce(f32[32,64]{1,0:T(8,128)S(1)} %fusion.53, f32[64]{0:T(128)S(1)} %get-tuple-element.41), channel_id=1, replica_groups=mesh['seq'=64,'chan'=2] {'seq','chan'}, use_global_device_ids=true, to_apply=%region_0.1 | all-reduce | flops 2112 | bytes 16896 | tf_op jit(solution)/shard_map/psum | solution.py:152
  325.1 5.9 all-to-all-start.3
  331.5 280.7 %psum.23 = f32[64,64]{1,0:T(8,128)S(1)} all-reduce(f32[64,64]{1,0:T(8,128)S(1)} %fusion.40), channel_id=1, replica_groups=mesh['seq'=64,'chan'=2] {'seq'}, use_global_device_ids=true, to_apply=%region_3.4 | all-reduce | flops 4096 | bytes 32768 | tf_op jit(solution)/shard_map/psum | solution.py:151
  (101 shorter events, 93.5 us)
Async XLA Ops:
  0.6 18.3 %copy-start = (f32[64,64]{1,0:T(8,128)S(1)}, f32[64,64]{1,0:T(8,128)}, u32[]{:S(2)}) copy-start(f32[64,64]{1,0:T(8,128)} %param.12) | copy-start | bytes 49156
  4.4 19.8 %all-to-all-start = ((bf16[64,2,1024]{2,1,0:T(2,128)(2,1)}), bf16[64,2,1024]{2,1,0:T(2,128)(2,1)S(1)}, u32[]{:S(2)}, u32[]{:S(2)}) async-start(bf16[64,2,1024]{2,1,0:T(2,128)(2,1)} %pad_maximum_fusion.14), calls=%async_computation | async-start | bytes 524288 | tf_op jit(solution)/shard_map/all_to_all | solution.py:60
  16.2 2.7 copy-start.13
  33.4 46.6 %all-to-all-start.1 = ((f32[128,2,3,1024]{3,1,2,0:T(2,128)}), f32[128,2,3,1024]{3,1,2,0:T(2,128)S(1)}, u32[]{:S(2)}, u32[]{:S(2)}) async-start(f32[128,2,3,1024]{3,1,2,0:T(2,128)} %copy.76), calls=%async_computation.1 | async-start | bytes 6291456 | tf_op jit(solution)/shard_map/all_to_all | solution.py:77
  41.2 0.6 copy-start.15
  109.9 5.5 copy-start.1
  110.0 5.5 copy-start.2
  110.0 5.5 copy-start.3
  126.2 6.8 %copy-start.6 = (f32[64,2,1,16,64]{4,3,2,1,0:T(8,128)}, f32[64,2,1,16,64]{4,3,2,1,0:T(8,128)S(1)}, u32[]{:S(2)}) copy-start(f32[64,2,1,16,64]{4,3,2,1,0:T(8,128)S(1)} %get-tuple-element.13) | copy-start | bytes 1572868
  126.9 6.0 copy-start.4
  126.9 6.0 copy-start.5
  148.9 4.6 copy-start.7
  148.9 4.6 copy-start.10
  148.9 4.6 copy-start.11
  171.9 7.0 %copy-start.8 = (f32[64,2,1024]{2,1,0:T(2,128)S(1)}, f32[64,2,1024]{2,1,0:T(2,128)}, u32[]{:S(2)}) copy-start(f32[64,2,1024]{2,1,0:T(2,128)} %get-tuple-element.25) | copy-start | bytes 1572868
  171.9 7.0 %copy-start.9 = (f32[64,2,1024]{2,1,0:T(2,128)S(1)}, f32[64,2,1024]{2,1,0:T(2,128)}, u32[]{:S(2)}) copy-start(f32[64,2,1024]{2,1,0:T(2,128)} %get-tuple-element.26) | copy-start | bytes 1572868
  187.5 46.3 %all-to-all-start.2 = ((f32[64,2,2,3,1024]{4,2,3,1,0:T(2,128)}), f32[64,2,2,3,1024]{4,2,3,1,0:T(2,128)S(1)}, u32[]{:S(2)}, u32[]{:S(2)}) async-start(f32[64,2,2,3,1024]{4,2,3,1,0:T(2,128)} %copy.86), calls=%async_computation.2 | async-start | bytes 6291456 | tf_op jit(solution)/shard_map/all_to_all | solution.py:135
  254.0 4.2 copy-start.12
  254.0 5.6 copy-start.14
  325.1 287.8 %all-to-all-start.3 = ((bf16[64,2,1024]{2,1,0:T(2,128)(2,1)}), bf16[64,2,1024]{2,1,0:T(2,128)(2,1)S(1)}, u32[]{:S(2)}, u32[]{:S(2)}) async-start(bf16[64,2,1024]{2,1,0:T(2,128)(2,1)} %slice.117), calls=%async_computation.3 | async-start | bytes 524288 | tf_op jit(solution)/shard_map/all_to_all | solution.py:140
where the time goes:
time: 627 us; the launch traced here: 616 us
  blocking collectives  345 us (55%)
  local copies, waits for them, and re-layouts  80.4 us (13%)
  waiting for transfers between devices  64.5 us (10%)
  matrix products  58.9 us (9%)
  other arithmetic  35.8 us (6%)
  starting transfers between devices  29.3 us (5%)
    psum x1, blocking collectives, local(): out_sum = lax.psum(out_part, 'seq')  281 us
    psum x1, blocking collectives, local(): embed_all, bias_all = lax.psum((embed_part, bias_part), ('seq', 'chan'))  64.6 us
    all_to_all x1, waiting for transfers between devices, local(): back = lax.all_to_all(back, 'seq', split_axis=0, concat_axis=0, tiled=True)  38.9 us
    dot_general x8, matrix products, blk_mix(): jnp.einsum('mb,qkzbc->qkzmc', table, vals, preferred_element_type=jnp.flo...  32.6 us
    dot_general x10, matrix products, mat_dot(): jnp.dot(lhs_mat, rhs_mat, preferred_element_type=jnp.float32, precision=e...  26.2 us
    all_to_all x1, waiting for transfers between devices, local(): spec = lax.all_to_all(spec, 'seq', split_axis=0, concat_axis=0, tiled=True)  23.2 us
  transfers between devices with their start and end apart: 4, of which 3 were waited for; matrix products, arithmetic and copies ran while one was open for 4% of the time, Pallas kernels for 0%

commit v1 on v0

--- a/solution.py
+++ b/solution.py
@@ -149,7 +149,7 @@
     embed_part = mat_dot(features.T, d_preact)
     bias_part = jnp.sum(d_preact, axis=0)
     out_sum = lax.psum(out_part, "seq")
-    embed_all, bias_all = lax.psum((embed_part, bias_part), ("seq", "chan"))
+    embed_all, bias_all = lax.psum(lax.psum((embed_part, bias_part), "seq"), "chan")
     norm_scale = 1.0 / math.sqrt(seq_total)
     return (conv_out, d_signal, embed_all * norm_scale, bias_all * norm_scale, out_sum * norm_scale)
 

time: 627 us -> 578 us (0.922)
  the two profiles are of different devices: /device:TPU:0 before, /device:TPU:1 now
where the time goes in v1:
time: 578 us; the launch traced here: 567 us
  blocking collectives  280 us (48%)
  local copies, waits for them, and re-layouts  80.5 us (14%)
  waiting for transfers between devices  73.5 us (13%)
  matrix products  58.9 us (10%)
  starting transfers between devices  36.7 us (6%)
  other arithmetic  35.8 us (6%)
    psum x1, blocking collectives, local(): lax.psum((embed_part, bias_part), 'seq')  270 us
    all_to_all x1, waiting for transfers between devices, local(): back = lax.all_to_all(back, 'seq', split_axis=0, concat_axis=0, tiled=True)  39.3 us
    dot_general x8, matrix products, blk_mix(): jnp.einsum('mb,qkzbc->qkzmc', table, vals, preferred_element_type=jnp.flo...  32.7 us
    dot_general x10, matrix products, mat_dot(): jnp.dot(lhs_mat, rhs_mat, preferred_element_type=jnp.float32, precision=e...  26.2 us
    all_to_all x1, waiting for transfers between devices, local(): spec = lax.all_to_all(spec, 'seq', split_axis=0, concat_axis=0, tiled=True)  23.7 us
    all_to_all x1, starting transfers between devices, local(): lax.all_to_all(res[:, 0:2].astype(jnp.bfloat16), 'seq', split_axis=0, con...  12.3 us
  transfers between devices with their start and end apart: 4, of which 4 were waited for; matrix products, arithmetic and copies ran while one was open for 4% of the time, Pallas kernels for 0%

profile of v1, /device:TPU:1, one launch (start us, length us, event | category | flops | bytes accessed | tf_op | source)
XLA Modules:
  0.0 566.8 jit_solution(1130801036788273230)
XLA Ops:
  4.4 10.8 %all-to-all-start = ((bf16[64,2,1024]{2,1,0:T(2,128)(2,1)}), bf16[64,2,1024]{2,1,0:T(2,128)(2,1)S(1)}, u32[]{:S(2)}, u32[]{:S(2)}) async-start(bf16[64,2,1024]{2,1,0:T(2,128)(2,1)} %pad_maximum_fusion.14), calls=%async_computation | async-start | bytes 524288 | tf_op jit(solution)/shard_map/all_to_all | solution.py:60
  29.9 4.1 copy.76
  34.0 7.2 %all-to-all-start.1 = ((f32[128,2,3,1024]{3,1,2,0:T(2,128)}), f32[128,2,3,1024]{3,1,2,0:T(2,128)S(1)}, u32[]{:S(2)}, u32[]{:S(2)}) async-start(f32[128,2,3,1024]{3,1,2,0:T(2,128)} %copy.76), calls=%async_computation.1 | async-start | bytes 6291456 | tf_op jit(solution)/shard_map/all_to_all | solution.py:77
  48.2 9.5 %fusion.38 = (f32[64,2,1024]{2,1,0:T(2,128)}, f32[64,2,1024]{2,1,0:T(2,128)}) fusion(s32[2]{0:T(128)S(1)} %iota_add_fusion.1, s32[64,1024]{1,0:T(8,128)S(1)} %broadcast_add_fusion), kind=kLoop, calls=%fused_computation.88 | loop fusion | flops 1835008 | bytes 1310728 | tf_op jit(solution)/shard_map/cos | solution.py:130
  57.7 23.7 %all-to-all-done.1 = f32[128,2,3,1024]{3,1,2,0:T(2,128)S(1)} async-done(((f32[128,2,3,1024]{3,1,2,0:T(2,128)}), f32[128,2,3,1024]{3,1,2,0:T(2,128)S(1)}, u32[]{:S(2)}, u32[]{:S(2)}) %all-to-all-start.1) | async-done | bytes 3145760 | tf_op jit(solution)/shard_map/all_to_all | solution.py:77
  85.1 4.3 reshape.397
  93.2 9.4 %fusion = f32[2,64,2,2,3,1024]{5,1,4,3,2,0:T(8,128)S(1)} fusion(f32[2,64,64,1,1,1]{2,1,5,4,3,0:T(8,128)} %bitcast.98, f32[2,2,3,1024,64]{3,2,1,0,4:T(4,128)} %dot_general.72), kind=kOutput, calls=%fused_computation.6 | convolution fusion | flops 1207959552 | bytes 9469952 | tf_op jit(solution)/shard_map/dot_general | solution.py:11
  111.4 5.5 fusion.51
  134.4 4.7 subtract_bitcast_fusion
  139.0 4.9 reshape.411
  143.9 6.4 %add_bitcast_fusion = f32[64,2,3,16,64]{4,3,2,1,0:T(8,128)} fusion(f32[64,2,3,64,16]{3,4,2,1,0:T(8,128)S(1)} %fusion.3, f32[64,2,1,16,64]{4,3,2,1,0:T(8,128)} %copy-done.5, f32[64,2,1,16,64]{4,3,2,1,0:T(8,128)} %copy-done.6, f32[64,2,1,16,64]{4,3,2,1,0:T(8,128)} %copy-done.4), kind=kOutput, calls=%fused_computation.9 | convolution fusion | flops 76680704 | bytes 4718592 | tf_op jit(solution)/shard_map/mb,qkzbc->qkzmc/dot_general | solution.py:91
  150.3 4.6 reshape.412
  158.6 4.1 copy.85
  162.7 5.0 reshape.400
  176.4 3.9 squeeze.5
  184.3 4.7 copy.86
  188.9 6.3 %all-to-all-start.2 = ((f32[64,2,2,3,1024]{4,2,3,1,0:T(2,128)}), f32[64,2,2,3,1024]{4,2,3,1,0:T(2,128)S(1)}, u32[]{:S(2)}, u32[]{:S(2)}) async-start(f32[64,2,2,3,1024]{4,2,3,1,0:T(2,128)} %copy.86), calls=%async_computation.2 | async-start | bytes 6291456 | tf_op jit(solution)/shard_map/all_to_all | solution.py:135
  196.0 39.3 %all-to-all-done.2 = f32[64,2,2,3,1024]{4,2,3,1,0:T(2,128)S(1)} async-done(((f32[64,2,2,3,1024]{4,2,3,1,0:T(2,128)}), f32[64,2,2,3,1024]{4,2,3,1,0:T(2,128)S(1)}, u32[]{:S(2)}, u32[]{:S(2)}) %all-to-all-start.2) | async-done | bytes 3145760 | tf_op jit(solution)/shard_map/all_to_all | solution.py:135
  238.9 5.0 reshape.401
  243.8 4.1 copy.88
  261.4 270.4 %all-reduce = (f32[32,64]{1,0:T(8,128)S(1)}, f32[64]{0:T(128)S(1)}, f32[64,64]{1,0:T(8,128)S(1)}) all-reduce(f32[32,64]{1,0:T(8,128)S(1)} %fusion.53, f32[64]{0:T(128)S(1)} %get-tuple-element.44, f32[64,64]{1,0:T(8,128)S(1)} %fusion.40), channel_id=1, replica_groups=mesh['seq'=64,'chan'=2] {'seq'}, use_global_device_ids=true, to_apply=%region_0.1 | all-reduce | flops 6208 | bytes 49664 | tf_op jit(solution)/shard_map/psum | solution.py:152
  531.8 9.4 %all-reduce.1 = (f32[32,64]{1,0:T(8,128)S(1)}, f32[64]{0:T(128)S(1)}) all-reduce(f32[32,64]{1,0:T(8,128)S(1)} %get-tuple-element.7, f32[64]{0:T(128)S(1)} %get-tuple-element.8), channel_id=1, replica_groups=mesh['seq'=64,'chan'=2] {'chan'}, use_global_device_ids=true, to_apply=%region_1.2 | all-reduce | flops 2112 | bytes 16896 | tf_op jit(solution)/shard_map/psum | solution.py:152
  541.9 12.3 %all-to-all-start.3 = ((bf16[64,2,1024]{2,1,0:T(2,128)(2,1)}), bf16[64,2,1024]{2,1,0:T(2,128)(2,1)S(1)}, u32[]{:S(2)}, u32[]{:S(2)}) async-start(bf16[64,2,1024]{2,1,0:T(2,128)(2,1)} %slice.117), calls=%async_computation.3 | async-start | bytes 524288 | tf_op jit(solution)/shard_map/all_to_all | solution.py:140
  555.3 8.6 %all-to-all-done.3 = bf16[64,2,1024]{2,1,0:T(2,128)(2,1)S(1)} async-done(((bf16[64,2,1024]{2,1,0:T(2,128)(2,1)}), bf16[64,2,1024]{2,1,0:T(2,128)(2,1)S(1)}, u32[]{:S(2)}, u32[]{:S(2)}) %all-to-all-start.3) | async-done | bytes 262176 | tf_op jit(solution)/shard_map/all_to_all | solution.py:140
  (101 shorter events, 97.1 us)
Async XLA Ops:
  0.6 19.2 %copy-start = (f32[64,64]{1,0:T(8,128)S(1)}, f32[64,64]{1,0:T(8,128)}, u32[]{:S(2)}) copy-start(f32[64,64]{1,0:T(8,128)} %param.12) | copy-start | bytes 49156
  4.4 20.4 %all-to-all-start = ((bf16[64,2,1024]{2,1,0:T(2,128)(2,1)}), bf16[64,2,1024]{2,1,0:T(2,128)(2,1)S(1)}, u32[]{:S(2)}, u32[]{:S(2)}) async-start(bf16[64,2,1024]{2,1,0:T(2,128)(2,1)} %pad_maximum_fusion.14), calls=%async_computation | async-start | bytes 524288 | tf_op jit(solution)/shard_map/all_to_all | solution.py:60
  17.2 2.7 copy-start.13
  34.0 47.4 %all-to-all-start.1 = ((f32[128,2,3,1024]{3,1,2,0:T(2,128)}), f32[128,2,3,1024]{3,1,2,0:T(2,128)S(1)}, u32[]{:S(2)}, u32[]{:S(2)}) async-start(f32[128,2,3,1024]{3,1,2,0:T(2,128)} %copy.76), calls=%async_computation.1 | async-start | bytes 6291456 | tf_op jit(solution)/shard_map/all_to_all | solution.py:77
  42.2 0.6 copy-start.15
  111.4 5.5 copy-start.1
  111.4 5.5 copy-start.2
  111.4 5.5 copy-start.3
  127.6 6.8 %copy-start.6 = (f32[64,2,1,16,64]{4,3,2,1,0:T(8,128)}, f32[64,2,1,16,64]{4,3,2,1,0:T(8,128)S(1)}, u32[]{:S(2)}) copy-start(f32[64,2,1,16,64]{4,3,2,1,0:T(8,128)S(1)} %get-tuple-element.16) | copy-start | bytes 1572868
  128.3 6.0 %copy-start.4 = (f32[64,2,1,16,64]{4,3,2,1,0:T(8,128)}, f32[64,2,1,16,64]{4,3,2,1,0:T(8,128)S(1)}, u32[]{:S(2)}) copy-start(f32[64,2,1,16,64]{4,3,2,1,0:T(8,128)S(1)} %get-tuple-element.12) | copy-start | bytes 1572868
  128.3 6.0 %copy-start.5 = (f32[64,2,1,16,64]{4,3,2,1,0:T(8,128)}, f32[64,2,1,16,64]{4,3,2,1,0:T(8,128)S(1)}, u32[]{:S(2)}) copy-start(f32[64,2,1,16,64]{4,3,2,1,0:T(8,128)S(1)} %get-tuple-element.13) | copy-start | bytes 1572868
  150.3 4.6 copy-start.7
  150.3 4.6 copy-start.10
  150.3 4.6 copy-start.11
  173.3 7.0 %copy-start.8 = (f32[64,2,1024]{2,1,0:T(2,128)S(1)}, f32[64,2,1024]{2,1,0:T(2,128)}, u32[]{:S(2)}) copy-start(f32[64,2,1024]{2,1,0:T(2,128)} %get-tuple-element.28) | copy-start | bytes 1572868
  173.3 7.0 %copy-start.9 = (f32[64,2,1024]{2,1,0:T(2,128)S(1)}, f32[64,2,1024]{2,1,0:T(2,128)}, u32[]{:S(2)}) copy-start(f32[64,2,1024]{2,1,0:T(2,128)} %get-tuple-element.29) | copy-start | bytes 1572868
  188.9 46.3 %all-to-all-start.2 = ((f32[64,2,2,3,1024]{4,2,3,1,0:T(2,128)}), f32[64,2,2,3,1024]{4,2,3,1,0:T(2,128)S(1)}, u32[]{:S(2)}, u32[]{:S(2)}) async-start(f32[64,2,2,3,1024]{4,2,3,1,0:T(2,128)} %copy.86), calls=%async_computation.2 | async-start | bytes 6291456 | tf_op jit(solution)/shard_map/all_to_all | solution.py:135
  255.4 4.2 copy-start.12
  255.4 5.6 copy-start.14
  541.9 22.0 %all-to-all-start.3 = ((bf16[64,2,1024]{2,1,0:T(2,128)(2,1)}), bf16[64,2,1024]{2,1,0:T(2,128)(2,1)S(1)}, u32[]{:S(2)}, u32[]{:S(2)}) async-start(bf16[64,2,1024]{2,1,0:T(2,128)(2,1)} %slice.117), calls=%async_computation.3 | async-start | bytes 524288 | tf_op jit(solution)/shard_map/all_to_all | solution.py:140
